TPU v7x, 512 devices: a whole 4x4x16 slice. The times are simulated.
512 devices in a mesh: dp: 32 (over x, y, core), expert: 16 (over z).
Axes of the slice: x: 4, y: 4, z: 16, core: 2. Of those that a mesh axis runs over, the one named last changes fastest.
Arguments:
- out_grad: bfloat16 [65536, 2048], P(('dp', 'expert')), may hold values from -6 to 6
- expert_ids: int32 [65536, 4], P(('dp', 'expert')), may hold values from 0 to 15, all different within a row; in each aligned block of 128 rows (0 to 127, 128 to 255, ...) at most 64 rows name the same one
- route_weights: bfloat16 [65536, 4], P(('dp', 'expert')), may hold values from 0.049804688 to 1
- pre_activations: bfloat16 [65536, 4, 1536], P(('dp', 'expert')), may hold values from -6 to 6
- down_weight: bfloat16 [16, 768, 2048], P('expert', 'dp'), may hold values from -0.21875 to 0.21875
Outputs:
- pre_grad: bfloat16 [65536, 4, 1536], P(('dp', 'expert'))
- weight_grad: bfloat16 [65536, 4], P(('dp', 'expert'))
- down_grad: bfloat16 [16, 768, 2048], P('expert', 'dp')
Inputs may be any that keep to these rules, and one draw needn't show every extreme that they name: `expert_ids`: among the 128 rows of one device, each expert is named by at most 64 rows, a bound that some block reaches; the numbers in a row are distinct.
All inputs are finite; a program needn't handle non-finite values.
Results may differ from a plain program's by a relative error of at most 0.015.
Values may be sent and summed in bfloat16 or wider, within the bound.
No kernel may reach another device: no remote copies, remote signals or barrier semaphores. Data moves between devices by JAX's collectives and lax.ppermute only.
A program may use at most 64 MiB of HBM per device.

v0:
```python
import jax
import jax.numpy as jnp
from jax import lax
from jax.sharding import PartitionSpec as P

F32 = jnp.float32
BF16 = jnp.bfloat16


def gather_rows(x):
    return lax.all_gather(x, "dp", axis=0, tiled=True)


def body(out_grad, expert_ids, route_weights, pre_activations, down_weight):
    tok, width = out_grad.shape
    top = expert_ids.shape[1]
    units = pre_activations.shape[2] // 2
    ndp = lax.axis_size("dp")
    rows = down_weight.shape[1]
    n_all = ndp * tok
    w_all = lax.all_gather(down_weight, "expert", axis=0, tiled=True)
    experts = w_all.shape[0]
    wcat = w_all.reshape(experts * rows, width)
    og_all = gather_rows(out_grad)
    ids_t = gather_rows(expert_ids).T
    rw_t = gather_rows(route_weights).T.astype(F32)
    gate = pre_activations[..., :units].astype(F32)
    up = pre_activations[..., units:].astype(F32)
    sig = jax.nn.sigmoid(gate)
    hidden = (gate * sig * up).astype(BF16)
    send_h = hidden.reshape(tok, top, ndp, rows).transpose(2, 0, 1, 3)
    got_h = lax.all_to_all(send_h, "dp", 0, 0, tiled=True)
    hid_t = got_h.transpose(2, 3, 0, 1).reshape(top, rows, n_all).astype(F32)
    eidx = jnp.arange(experts, dtype=jnp.int32)[:, None, None]
    hp = jnp.zeros((experts, rows, n_all), F32)
    for k in range(top):
        hp = hp + jnp.where(
            ids_t[k][None, None, :] == eidx, (rw_t[k][None, :] * hid_t[k])[None], 0.0
        )
    hp = hp.reshape(experts * rows, n_all).astype(BF16)
    part = lax.dot_general(hp, og_all, (((1,), (0,)), ((), ())), preferred_element_type=F32)
    r_t = lax.dot_general(wcat, og_all, (((1,), (1,)), ((), ())), preferred_element_type=F32)
    r_t = r_t.reshape(experts, rows, n_all)
    hg_t = jnp.stack(
        [jnp.sum(jnp.where(ids_t[k][None, None, :] == eidx, r_t, 0.0), axis=0) for k in range(top)]
    ).astype(BF16)
    send_g = hg_t.reshape(top, rows, ndp, tok).transpose(2, 3, 0, 1)
    got_g = lax.all_to_all(send_g, "dp", 0, 0, tiled=True)
    hidden_grad = got_g.transpose(1, 2, 0, 3).reshape(tok, top, units)
    hg32 = hidden_grad.astype(F32)
    weight_grad = jnp.sum(hg32 * hidden.astype(F32), axis=-1).astype(BF16)
    cot = route_weights.astype(F32)[..., None] * hg32
    gate_grad = cot * up * sig * (1.0 + gate * (1.0 - sig))
    up_grad = cot * gate * sig
    pre_grad = jnp.concatenate([gate_grad, up_grad], axis=-1).astype(BF16)
    summed = lax.psum_scatter(
        part.reshape(experts, rows, width).astype(BF16), "expert", scatter_dimension=0, tiled=True
    )
    down_grad = (summed.astype(F32) / ndp).astype(BF16)
    return (pre_grad, weight_grad, down_grad)


def solution(mesh):
    return jax.shard_map(
        body,
        mesh=mesh,
        in_specs=(
            P(("dp", "expert"), None),
            P(("dp", "expert"), None),
            P(("dp", "expert"), None),
            P(("dp", "expert"), None, None),
            P("expert", "dp", None),
        ),
        out_specs=(
            P(("dp", "expert"), None, None),
            P(("dp", "expert"), None),
            P("expert", "dp", None),
        ),
        check_vma=False,
    )
```

profile of v0, /device:TPU:4, one launch (start us, length us, event | category | flops | bytes accessed | tf_op | source)
XLA Modules:
  0.0 325.2 jit_solution(932634305599170821)
XLA Ops:
  7.2 0.7 all-gather.3.cloned.1.call-update
  7.9 0.7 all-gather.5.cloned.1.call-update
  8.6 1.9 fusion.30
  10.6 0.7 copy.37
  11.3 0.7 copy.36
  12.0 24.4 %all_gather.15 = bf16[4096,4]{0,1:T(4,128)(2,1)S(1)} all-gather(bf16[128,4]{0,1:T(4,128)(2,1)S(1)} %copy-done.1), channel_id=1, replica_groups=mesh['dp'=32,'expert'=16] {'dp'}, dimensions={0}, use_global_device_ids=true | all-gather | bytes 33792 | tf_op jit(solution)/shard_map/all_gather | solution.py:11
  36.4 24.9 %all_gather.12 = s32[4096,4]{0,1:T(4,128)S(1)} all-gather(s32[128,4]{0,1:T(4,128)S(1)} %copy-done.2), channel_id=1, replica_groups=mesh['dp'=32,'expert'=16] {'dp'}, dimensions={0}, use_global_device_ids=true | all-gather | bytes 67584 | tf_op jit(solution)/shard_map/all_gather | solution.py:11
  61.5 24.7 %all-gather.3.cloned.1.call-done = bf16[16,24,2048]{2,1,0:T(8,128)(2,1)} async-done(((bf16[1,24,2048]{2,1,0:T(8,128)(2,1)}), bf16[16,24,2048]{2,1,0:T(8,128)(2,1)}) %all-gather.3.cloned.1.call-update) | async-done | bytes 1572880 | tf_op jit(solution)/shard_map/all_gather | solution.py:21
  86.3 88.2 %all-gather.5.cloned.1.call-done = bf16[4096,2048]{1,0:T(8,128)(2,1)} async-done(((bf16[128,2048]{1,0:T(8,128)(2,1)}), bf16[4096,2048]{1,0:T(8,128)(2,1)}) %all-gather.5.cloned.1.call-update) | async-done | bytes 16777232 | tf_op jit(solution)/shard_map/all_gather | solution.py:11
  174.5 12.7 %select_reduce_fusion.3 = (bf16[24,4096]{1,0:T(8,128)(2,1)S(1)}, bf16[24,4096]{1,0:T(8,128)(2,1)S(1)}, bf16[24,4096]{1,0:T(8,128)(2,1)S(1)}, bf16[24,4096]{1,0:T(8,128)(2,1)S(1)}) fusion(pred[16,4096]{1,0:T(8,128)(4,1)S(1)} %get-tuple-element.37, pred[16,4096]{1,0:T(8,128)(4,1)S(1)} %get-tuple-element.34, pred[16,4096]{1,0:T(8,128)(4,1)S(1)} %get-tuple-element.35, ...), kind=kOutput, calls=%fused_computation.8 | convolution fusion | flops 6454640640 | bytes 19398656 | tf_op jit(solution)/shard_map/dot_general | solution.py:42
  187.5 1.2 copy.25
  188.7 5.7 %all-to-all-start = ((bf16[32,128,4,24]{1,3,2,0:T(8,128)(2,1)}), bf16[32,128,4,24]{1,3,2,0:T(8,128)(2,1)S(1)}, u32[]{:S(2)}, u32[]{:S(2)}) async-start(bf16[32,128,4,24]{1,3,2,0:T(8,128)(2,1)} %copy.25), calls=%async_computation | async-start | bytes 1572864 | tf_op jit(solution)/shard_map/all_to_all | solution.py:48
  194.4 12.1 %all-to-all-done = bf16[32,128,4,24]{1,3,2,0:T(8,128)(2,1)S(1)} async-done(((bf16[32,128,4,24]{1,3,2,0:T(8,128)(2,1)}), bf16[32,128,4,24]{1,3,2,0:T(8,128)(2,1)S(1)}, u32[]{:S(2)}, u32[]{:S(2)}) %all-to-all-start) | async-done | bytes 786464 | tf_op jit(solution)/shard_map/all_to_all | solution.py:48
  206.5 2.6 fusion.26
  209.1 1.0 copy.29
  210.1 5.9 %all-to-all-start.1 = ((bf16[32,128,4,24]{1,3,2,0:T(8,128)(2,1)}), bf16[32,128,4,24]{1,3,2,0:T(8,128)(2,1)S(1)}, u32[]{:S(2)}, u32[]{:S(2)}) async-start(bf16[32,128,4,24]{1,3,2,0:T(8,128)(2,1)} %copy.29), calls=%async_computation.1 | async-start | bytes 1572864 | tf_op jit(solution)/shard_map/all_to_all | solution.py:32
  216.0 0.2 reduce-scatter.2.cloned.1.call-start
  216.3 11.8 %all-to-all-done.1 = bf16[32,128,4,24]{1,3,2,0:T(8,128)(2,1)S(1)} async-done(((bf16[32,128,4,24]{1,3,2,0:T(8,128)(2,1)}), bf16[32,128,4,24]{1,3,2,0:T(8,128)(2,1)S(1)}, u32[]{:S(2)}, u32[]{:S(2)}) %all-to-all-start.1) | async-done | bytes 786464 | tf_op jit(solution)/shard_map/all_to_all | solution.py:32
  228.1 0.3 convert_bitcast_fusion
  228.5 0.3 broadcast_multiply_fusion
  228.8 0.2 copy.50
  229.1 0.3 broadcast_multiply_fusion.1
  229.4 0.2 copy.51
  229.6 0.3 broadcast_multiply_fusion.2
  229.9 0.2 copy.52
  230.2 0.3 broadcast_multiply_fusion.3
  230.5 0.2 copy.53
  230.8 13.7 %fusion.13 = bf16[16,24,2048]{2,1,0:T(8,128)(2,1)} fusion(bf16[4096,2048]{1,0:T(8,128)(2,1)} %all-gather.5.cloned.1.call-done, f32[24,4096]{1,0:T(8,128)S(1)} %bitcast.84, f32[24,4096]{1,0:T(8,128)S(1)} %bitcast.85, f32[24,4096]{1,0:T(8,128)S(1)} %bitcast.86, f32[24,4096]{1,0:T(8,128)S(1)} %bitcast.87, pred[16,4096]{1,0:T(8,128)(4,1)S(1)} %get-tuple-element.34, ...), kind=kOutput, calls=%fused_computation.18 | convolution fusion | flops 6455820288 | bytes 20185088 | tf_op jit(solution)/shard_map/dot_general | solution.py:41
  244.5 1.1 copy-done
  245.7 2.5 copy.31
  248.2 69.0 %reduce-scatter.2.cloned.1.call-done = bf16[1,24,2048]{2,1,0:T(8,128)(2,1)} async-done(((bf16[16,24,2048]{2,1,0:T(8,128)(2,1)}), bf16[1,24,2048]{2,1,0:T(8,128)(2,1)}) %reduce-scatter.2.cloned.1.call-update) | async-done | bytes 98320 | tf_op jit(solution)/shard_map/reduce_scatter | solution.py:56
  317.1 1.6 multiply_convert_fusion
  (21 shorter events, 0.8 us)
Async XLA Ops:
  7.2 79.1 %all-gather.3.cloned.1.call-start = ((), (), s32[]{:S(2)}) async-start(), calls=%async_computation.3 | async-start | bytes 1671168 | tf_op jit(solution)/shard_map/all_gather | solution.py:21
  7.9 166.6 %all-gather.5.cloned.1.call-start = ((), (), s32[]{:S(2)}) async-start(), calls=%async_computation.4 | async-start | bytes 17301504 | tf_op jit(solution)/shard_map/all_gather | solution.py:11
  10.6 1.4 copy-start.1
  10.6 25.8 %copy-start.2 = (s32[128,4]{0,1:T(4,128)S(1)}, s32[128,4]{0,1:T(4,128)}, u32[]{:S(2)}) copy-start(s32[128,4]{0,1:T(4,128)} %param.6) | copy-start | bytes 6148
  188.7 17.8 %all-to-all-start = ((bf16[32,128,4,24]{1,3,2,0:T(8,128)(2,1)}), bf16[32,128,4,24]{1,3,2,0:T(8,128)(2,1)S(1)}, u32[]{:S(2)}, u32[]{:S(2)}) async-start(bf16[32,128,4,24]{1,3,2,0:T(8,128)(2,1)} %copy.25), calls=%async_computation | async-start | bytes 1572864 | tf_op jit(solution)/shard_map/all_to_all | solution.py:48
  210.1 18.0 %all-to-all-start.1 = ((bf16[32,128,4,24]{1,3,2,0:T(8,128)(2,1)}), bf16[32,128,4,24]{1,3,2,0:T(8,128)(2,1)S(1)}, u32[]{:S(2)}, u32[]{:S(2)}) async-start(bf16[32,128,4,24]{1,3,2,0:T(8,128)(2,1)} %copy.29), calls=%async_computation.1 | async-start | bytes 1572864 | tf_op jit(solution)/shard_map/all_to_all | solution.py:32
  216.0 101.1 %reduce-scatter.2.cloned.1.call-start = ((), (), s32[]{:S(2)}) async-start(), calls=%async_computation.5 | async-start | bytes 1671168 | tf_op jit(solution)/shard_map/reduce_scatter | solution.py:56
  244.4 1.1 copy-start
Sparse Core Ops, SparseCore 0:
  10.1 76.1 all-gather.2
  89.4 85.0 all-gather.4
  244.6 72.4 reduce-scatter.1
where the time goes:
time: 326 us; the launch traced here: 325 us
  waiting for transfers between devices  207 us (63%)
  blocking collectives  49.4 us (15%)
  matrix products  26.4 us (8%)
  between operations  14 us (4%)
  starting transfers between devices  11.9 us (4%)
  local copies, waits for them, and re-layouts  10.3 us (3%)
  other arithmetic  6.07 us (2%)
    all_gather x1, waiting for transfers between devices, gather_rows(): return lax.all_gather(x, 'dp', axis=0, tiled=True)  88.2 us
    reduce_scatter x1, waiting for transfers between devices, body(): lax.psum_scatter(part.reshape(experts, rows, width).astype(BF16), 'expert...  69 us
    all_gather x2, blocking collectives, gather_rows(): return lax.all_gather(x, 'dp', axis=0, tiled=True)  49.4 us
    all_gather x1, waiting for transfers between devices, body(): w_all = lax.all_gather(down_weight, 'expert', axis=0, tiled=True)  24.7 us
    dot_general x1, matrix products, body(): lax.dot_general(hp, og_all, (((1,), (0,)), ((), ())), preferred_element_t...  13.7 us
    dot_general x1, matrix products, body(): lax.dot_general(wcat, og_all, (((1,), (1,)), ((), ())), preferred_element...  12.7 us
    all_to_all x1, waiting for transfers between devices, body(): got_g = lax.all_to_all(send_g, 'dp', 0, 0, tiled=True)  12.1 us
    all_to_all x1, waiting for transfers between devices, body(): got_h = lax.all_to_all(send_h, 'dp', 0, 0, tiled=True)  11.8 us
  transfers between devices with their start and end apart: 5, of which 5 were waited for; matrix products, arithmetic and copies ran while one was open for 2% of the time, Pallas kernels for 0%

commit v1 on v0

--- a/solution.py
+++ b/solution.py
@@ -18,7 +18,31 @@
     ndp = lax.axis_size("dp")
     rows = down_weight.shape[1]
     n_all = ndp * tok
-    w_all = lax.all_gather(down_weight, "expert", axis=0, tiled=True)
+    item_now, aux, u_next = (
+        lax.axis_size("expert"),
+        lax.axis_index("expert"),
+        down_weight.shape[0],
+    )
+    gallery = [(b, (b + 1) % item_now) for b in range(item_now)]
+    cards = [(b, (b - 1) % item_now) for b in range(item_now)]
+    w_all = jnp.zeros(
+        (*down_weight.shape[:0], item_now * u_next, *down_weight.shape[1:]), down_weight.dtype
+    )
+    left_arr = outcome_arr = down_weight
+    w_all = lax.dynamic_update_slice_in_dim(w_all, down_weight, aux * u_next, axis=0)
+    a_next = item_now // 2
+    t = 1
+    while t < a_next + 1:
+        left_arr = lax.ppermute(left_arr, "expert", perm=gallery)
+        w_all = lax.dynamic_update_slice_in_dim(
+            w_all, left_arr, (aux - t) % item_now * u_next, axis=0
+        )
+        if t < item_now - a_next:
+            outcome_arr = lax.ppermute(outcome_arr, "expert", cards)
+            w_all = lax.dynamic_update_slice_in_dim(
+                w_all, outcome_arr, (aux + t) % item_now * u_next, axis=0
+            )
+        t = t + 1
     experts = w_all.shape[0]
     wcat = w_all.reshape(experts * rows, width)
     og_all = gather_rows(out_grad)

time: 326 us -> 281 us (0.86)
  the two profiles are of different devices: /device:TPU:4 before, /device:TPU:2 now
where the time goes in v1:
time: 281 us; the launch traced here: 280 us
  waiting for transfers between devices  94.6 us (34%)
  starting transfers between devices  70.1 us (25%)
  blocking collectives  46.7 us (17%)
  matrix products  26.3 us (9%)
  local copies, waits for them, and re-layouts  22 us (8%)
  between operations  14.6 us (5%)
  other arithmetic  6.06 us (2%)
    reduce_scatter x1, waiting for transfers between devices, body(): lax.psum_scatter(part.reshape(experts, rows, width).astype(BF16), 'expert...  65.6 us
    all_gather x2, blocking collectives, gather_rows(): return lax.all_gather(x, 'dp', axis=0, tiled=True)  46.7 us
    ppermute x7, starting transfers between devices, body(): outcome_arr = lax.ppermute(outcome_arr, 'expert', cards)  40.3 us
    ppermute x8, starting transfers between devices, body(): left_arr = lax.ppermute(left_arr, 'expert', perm=gallery)  17.2 us
    dot_general x1, matrix products, body(): lax.dot_general(hp, og_all, (((1,), (0,)), ((), ())), preferred_element_t...  13.6 us
    dot_general x1, matrix products, body(): lax.dot_general(wcat, og_all, (((1,), (1,)), ((), ())), preferred_element...  12.7 us
    all_to_all x1, waiting for transfers between devices, body(): got_g = lax.all_to_all(send_g, 'dp', 0, 0, tiled=True)  12 us
    all_to_all x1, waiting for transfers between devices, body(): got_h = lax.all_to_all(send_h, 'dp', 0, 0, tiled=True)  11.8 us
  transfers between devices with their start and end apart: 19, of which 4 were waited for; matrix products, arithmetic and copies ran while one was open for 6% of the time, Pallas kernels for 0%

profile of v1, /device:TPU:2, one launch (start us, length us, event | category | flops | bytes accessed | tf_op | source)
XLA Modules:
  0.0 280.5 jit_solution(1505820887417585490)
XLA Ops:
  7.9 3.8 %collective-permute-start = (bf16[1,24,2048]{2,1,0:T(8,128)(2,1)}, bf16[1,24,2048]{2,1,0:T(8,128)(2,1)S(1)}, u32[]{:S(2)}, u32[]{:S(2)}) collective-permute-start(bf16[1,24,2048]{2,1,0:T(8,128)(2,1)} %param.9), channel_id=1, source_target_pairs={{0,1},{1,2},{2,3},{3,4},{4,5},{5,6},{6,7},{7,8},{8,9},{9,10},{10,1... | collective-permute-start | bytes 294920 | tf_op jit(solution)/shard_map/ppermute | solution.py:36
  11.7 9.5 %collective-permute-start.1 = (bf16[1,24,2048]{2,1,0:T(8,128)(2,1)}, bf16[1,24,2048]{2,1,0:T(8,128)(2,1)S(1)}, u32[]{:S(2)}, u32[]{:S(2)}) collective-permute-start(bf16[1,24,2048]{2,1,0:T(8,128)(2,1)} %param.9), channel_id=1, source_target_pairs={{0,15},{1,0},{2,1},{3,2},{4,3},{5,4},{6,5},{7,6},{8,7},{9,8},{10,9... | collective-permute-start | bytes 294920 | tf_op jit(solution)/shard_map/ppermute | solution.py:41
  21.2 24.3 %all_gather.9 = s32[4096,4]{0,1:T(4,128)S(1)} all-gather(s32[128,4]{0,1:T(4,128)} %param.6), channel_id=1, replica_groups=mesh['dp'=32,'expert'=16] {'dp'}, dimensions={0}, use_global_device_ids=true | all-gather | bytes 67584 | tf_op jit(solution)/shard_map/all_gather | solution.py:11
  45.5 1.9 fusion.30
  47.7 1.3 broadcast_in_dim.91
  51.1 22.5 %all_gather.11 = bf16[4096,4]{0,1:T(4,128)(2,1)S(1)} all-gather(bf16[128,4]{0,1:T(4,128)(2,1)S(1)} %copy-done.4), channel_id=1, replica_groups=mesh['dp'=32,'expert'=16] {'dp'}, dimensions={0}, use_global_device_ids=true | all-gather | bytes 33792 | tf_op jit(solution)/shard_map/all_gather | solution.py:11
  73.6 1.9 collective-permute-start.2
  75.5 5.1 %collective-permute-start.3 = (bf16[1,24,2048]{2,1,0:T(8,128)(2,1)S(1)}, bf16[1,24,2048]{2,1,0:T(8,128)(2,1)S(1)}, u32[]{:S(2)}, u32[]{:S(2)}) collective-permute-start(bf16[1,24,2048]{2,1,0:T(8,128)(2,1)S(1)} %collective-permute-done.1), channel_id=1, source_target_pairs={{0,15},{1,0},{2,1},{3,2},{4,3},{5,4},{6,5},{7,6},{8,7},{9,8},{10,9... | collective-permute-start | bytes 294920 | tf_op jit(solution)/shard_map/ppermute | solution.py:41
  81.9 1.9 collective-permute-start.4
  83.9 5.1 %collective-permute-start.5 = (bf16[1,24,2048]{2,1,0:T(8,128)(2,1)S(1)}, bf16[1,24,2048]{2,1,0:T(8,128)(2,1)S(1)}, u32[]{:S(2)}, u32[]{:S(2)}) collective-permute-start(bf16[1,24,2048]{2,1,0:T(8,128)(2,1)S(1)} %collective-permute-done.3), channel_id=1, source_target_pairs={{0,15},{1,0},{2,1},{3,2},{4,3},{5,4},{6,5},{7,6},{8,7},{9,8},{10,9... | collective-permute-start | bytes 294920 | tf_op jit(solution)/shard_map/ppermute | solution.py:41
  90.3 1.9 collective-permute-start.6
  92.2 5.1 %collective-permute-start.7 = (bf16[1,24,2048]{2,1,0:T(8,128)(2,1)S(1)}, bf16[1,24,2048]{2,1,0:T(8,128)(2,1)S(1)}, u32[]{:S(2)}, u32[]{:S(2)}) collective-permute-start(bf16[1,24,2048]{2,1,0:T(8,128)(2,1)S(1)} %collective-permute-done.5), channel_id=1, source_target_pairs={{0,15},{1,0},{2,1},{3,2},{4,3},{5,4},{6,5},{7,6},{8,7},{9,8},{10,9... | collective-permute-start | bytes 294920 | tf_op jit(solution)/shard_map/ppermute | solution.py:41
  98.7 1.9 collective-permute-start.8
  100.6 5.1 %collective-permute-start.9 = (bf16[1,24,2048]{2,1,0:T(8,128)(2,1)S(1)}, bf16[1,24,2048]{2,1,0:T(8,128)(2,1)S(1)}, u32[]{:S(2)}, u32[]{:S(2)}) collective-permute-start(bf16[1,24,2048]{2,1,0:T(8,128)(2,1)S(1)} %collective-permute-done.7), channel_id=1, source_target_pairs={{0,15},{1,0},{2,1},{3,2},{4,3},{5,4},{6,5},{7,6},{8,7},{9,8},{10,9... | collective-permute-start | bytes 294920 | tf_op jit(solution)/shard_map/ppermute | solution.py:41
  107.1 1.9 collective-permute-start.10
  109.0 5.1 %collective-permute-start.11 = (bf16[1,24,2048]{2,1,0:T(8,128)(2,1)S(1)}, bf16[1,24,2048]{2,1,0:T(8,128)(2,1)S(1)}, u32[]{:S(2)}, u32[]{:S(2)}) collective-permute-start(bf16[1,24,2048]{2,1,0:T(8,128)(2,1)S(1)} %collective-permute-done.9), channel_id=1, source_target_pairs={{0,15},{1,0},{2,1},{3,2},{4,3},{5,4},{6,5},{7,6},{8,7},{9,8},{10,9... | collective-permute-start | bytes 294920 | tf_op jit(solution)/shard_map/ppermute | solution.py:41
  115.4 1.9 collective-permute-start.12
  117.4 5.1 %collective-permute-start.13 = (bf16[1,24,2048]{2,1,0:T(8,128)(2,1)S(1)}, bf16[1,24,2048]{2,1,0:T(8,128)(2,1)S(1)}, u32[]{:S(2)}, u32[]{:S(2)}) collective-permute-start(bf16[1,24,2048]{2,1,0:T(8,128)(2,1)S(1)} %collective-permute-done.11), channel_id=1, source_target_pairs={{0,15},{1,0},{2,1},{3,2},{4,3},{5,4},{6,5},{7,6},{8,7},{9,8},{10,9... | collective-permute-start | bytes 294920 | tf_op jit(solution)/shard_map/ppermute | solution.py:41
  123.8 1.9 collective-permute-start.14
  127.0 4.5 %collective-permute-done.14 = bf16[1,24,2048]{2,1,0:T(8,128)(2,1)S(1)} collective-permute-done((bf16[1,24,2048]{2,1,0:T(8,128)(2,1)S(1)}, bf16[1,24,2048]{2,1,0:T(8,128)(2,1)S(1)}, u32[]{:S(2)}, u32[]{:S(2)}) %collective-permute-start.14) | collective-permute-done | bytes 98336 | tf_op jit(solution)/shard_map/ppermute | solution.py:36
  132.2 12.7 %select_reduce_fusion.3 = (bf16[24,4096]{1,0:T(8,128)(2,1)S(1)}, bf16[24,4096]{1,0:T(8,128)(2,1)S(1)}, bf16[24,4096]{1,0:T(8,128)(2,1)S(1)}, bf16[24,4096]{1,0:T(8,128)(2,1)S(1)}) fusion(pred[16,4096]{1,0:T(8,128)(4,1)S(1)} %get-tuple-element.37, pred[16,4096]{1,0:T(8,128)(4,1)S(1)} %get-tuple-element.34, pred[16,4096]{1,0:T(8,128)(4,1)S(1)} %get-tuple-element.35, ...), kind=kOutput, calls=%fused_computation.8 | convolution fusion | flops 6454640640 | bytes 19398656 | tf_op jit(solution)/shard_map/dot_general | solution.py:66
  145.2 1.2 copy.25
  146.4 6.4 %all-to-all-start = ((bf16[32,128,4,24]{1,3,2,0:T(8,128)(2,1)}), bf16[32,128,4,24]{1,3,2,0:T(8,128)(2,1)S(1)}, u32[]{:S(2)}, u32[]{:S(2)}) async-start(bf16[32,128,4,24]{1,3,2,0:T(8,128)(2,1)} %copy.25), calls=%async_computation | async-start | bytes 1572864 | tf_op jit(solution)/shard_map/all_to_all | solution.py:72
  152.8 12.0 %all-to-all-done = bf16[32,128,4,24]{1,3,2,0:T(8,128)(2,1)S(1)} async-done(((bf16[32,128,4,24]{1,3,2,0:T(8,128)(2,1)}), bf16[32,128,4,24]{1,3,2,0:T(8,128)(2,1)S(1)}, u32[]{:S(2)}, u32[]{:S(2)}) %all-to-all-start) | async-done | bytes 786464 | tf_op jit(solution)/shard_map/all_to_all | solution.py:72
  164.8 2.6 fusion.26
  168.4 6.0 %all-to-all-start.1 = ((bf16[32,128,4,24]{1,3,2,0:T(8,128)(2,1)}), bf16[32,128,4,24]{1,3,2,0:T(8,128)(2,1)S(1)}, u32[]{:S(2)}, u32[]{:S(2)}) async-start(bf16[32,128,4,24]{1,3,2,0:T(8,128)(2,1)} %copy.29), calls=%async_computation.1 | async-start | bytes 1572864 | tf_op jit(solution)/shard_map/all_to_all | solution.py:56
  174.7 11.8 %all-to-all-done.1 = bf16[32,128,4,24]{1,3,2,0:T(8,128)(2,1)S(1)} async-done(((bf16[32,128,4,24]{1,3,2,0:T(8,128)(2,1)}), bf16[32,128,4,24]{1,3,2,0:T(8,128)(2,1)S(1)}, u32[]{:S(2)}, u32[]{:S(2)}) %all-to-all-start.1) | async-done | bytes 786464 | tf_op jit(solution)/shard_map/all_to_all | solution.py:56
  189.2 13.6 %fusion.13 = bf16[16,24,2048]{2,1,0:T(8,128)(2,1)} fusion(bf16[4096,2048]{1,0:T(8,128)(2,1)} %all-gather.2.cloned.1.call-done, f32[24,4096]{1,0:T(8,128)S(1)} %bitcast.84, f32[24,4096]{1,0:T(8,128)S(1)} %bitcast.85, f32[24,4096]{1,0:T(8,128)S(1)} %bitcast.86, f32[24,4096]{1,0:T(8,128)S(1)} %bitcast.87, pred[16,4096]{1,0:T(8,128)(4,1)S(1)} %get-tuple-element.34, ...), kind=kOutput, calls=%fused_computation.18 | convolution fusion | flops 6455820288 | bytes 20185088 | tf_op jit(solution)/shard_map/dot_general | solution.py:65
  202.8 1.1 copy-done
  204.0 2.5 copy.31
  206.5 65.6 %reduce-scatter.2.cloned.1.call-done = bf16[1,24,2048]{2,1,0:T(8,128)(2,1)} async-done(((bf16[16,24,2048]{2,1,0:T(8,128)(2,1)}), bf16[1,24,2048]{2,1,0:T(8,128)(2,1)}) %reduce-scatter.2.cloned.1.call-update) | async-done | bytes 98320 | tf_op jit(solution)/shard_map/reduce_scatter | solution.py:80
  272.1 1.6 multiply_convert_fusion
  (69 shorter events, 16.9 us)
Async XLA Ops:
  7.2 125.0 %all-gather.2.cloned.1.call-start = ((), (), s32[]{:S(2)}) async-start(), calls=%async_computation.3 | async-start | bytes 17301504 | tf_op jit(solution)/shard_map/all_gather | solution.py:11
  7.9 65.7 %collective-permute-start = (bf16[1,24,2048]{2,1,0:T(8,128)(2,1)}, bf16[1,24,2048]{2,1,0:T(8,128)(2,1)S(1)}, u32[]{:S(2)}, u32[]{:S(2)}) collective-permute-start(bf16[1,24,2048]{2,1,0:T(8,128)(2,1)} %param.9), channel_id=1, source_target_pairs={{0,1},{1,2},{2,3},{3,4},{4,5},{5,6},{6,7},{7,8},{8,9},{9,10},{10,1... | collective-permute-start | bytes 294920 | tf_op jit(solution)/shard_map/ppermute | solution.py:36
  11.7 63.8 %collective-permute-start.1 = (bf16[1,24,2048]{2,1,0:T(8,128)(2,1)}, bf16[1,24,2048]{2,1,0:T(8,128)(2,1)S(1)}, u32[]{:S(2)}, u32[]{:S(2)}) collective-permute-start(bf16[1,24,2048]{2,1,0:T(8,128)(2,1)} %param.9), channel_id=1, source_target_pairs={{0,15},{1,0},{2,1},{3,2},{4,3},{5,4},{6,5},{7,6},{8,7},{9,8},{10,9... | collective-permute-start | bytes 294920 | tf_op jit(solution)/shard_map/ppermute | solution.py:41
  47.4 1.6 copy-start.1
  47.7 84.5 %copy-start.2 = (pred[16,4096]{1,0:T(8,128)(4,1)}, pred[16,4096]{1,0:T(8,128)(4,1)S(1)}, u32[]{:S(2)}) copy-start(pred[16,4096]{1,0:T(8,128)(4,1)S(1)} %get-tuple-element.35) | copy-start | bytes 196612
  49.7 1.3 copy-start.4
  73.6 8.4 %collective-permute-start.2 = (bf16[1,24,2048]{2,1,0:T(8,128)(2,1)S(1)}, bf16[1,24,2048]{2,1,0:T(8,128)(2,1)S(1)}, u32[]{:S(2)}, u32[]{:S(2)}) collective-permute-start(bf16[1,24,2048]{2,1,0:T(8,128)(2,1)S(1)} %collective-permute-done), channel_id=1, source_target_pairs={{0,1},{1,2},{2,3},{3,4},{4,5},{5,6},{6,7},{7,8},{8,9},{9,10},{10,1... | collective-permute-start | bytes 294920 | tf_op jit(solution)/shard_map/ppermute | solution.py:36
  75.5 8.4 %collective-permute-start.3 = (bf16[1,24,2048]{2,1,0:T(8,128)(2,1)S(1)}, bf16[1,24,2048]{2,1,0:T(8,128)(2,1)S(1)}, u32[]{:S(2)}, u32[]{:S(2)}) collective-permute-start(bf16[1,24,2048]{2,1,0:T(8,128)(2,1)S(1)} %collective-permute-done.1), channel_id=1, source_target_pairs={{0,15},{1,0},{2,1},{3,2},{4,3},{5,4},{6,5},{7,6},{8,7},{9,8},{10,9... | collective-permute-start | bytes 294920 | tf_op jit(solution)/shard_map/ppermute | solution.py:41
  81.9 8.4 %collective-permute-start.4 = (bf16[1,24,2048]{2,1,0:T(8,128)(2,1)S(1)}, bf16[1,24,2048]{2,1,0:T(8,128)(2,1)S(1)}, u32[]{:S(2)}, u32[]{:S(2)}) collective-permute-start(bf16[1,24,2048]{2,1,0:T(8,128)(2,1)S(1)} %collective-permute-done.2), channel_id=1, source_target_pairs={{0,1},{1,2},{2,3},{3,4},{4,5},{5,6},{6,7},{7,8},{8,9},{9,10},{10,1... | collective-permute-start | bytes 294920 | tf_op jit(solution)/shard_map/ppermute | solution.py:36
  83.9 8.4 %collective-permute-start.5 = (bf16[1,24,2048]{2,1,0:T(8,128)(2,1)S(1)}, bf16[1,24,2048]{2,1,0:T(8,128)(2,1)S(1)}, u32[]{:S(2)}, u32[]{:S(2)}) collective-permute-start(bf16[1,24,2048]{2,1,0:T(8,128)(2,1)S(1)} %collective-permute-done.3), channel_id=1, source_target_pairs={{0,15},{1,0},{2,1},{3,2},{4,3},{5,4},{6,5},{7,6},{8,7},{9,8},{10,9... | collective-permute-start | bytes 294920 | tf_op jit(solution)/shard_map/ppermute | solution.py:41
  90.3 8.4 %collective-permute-start.6 = (bf16[1,24,2048]{2,1,0:T(8,128)(2,1)S(1)}, bf16[1,24,2048]{2,1,0:T(8,128)(2,1)S(1)}, u32[]{:S(2)}, u32[]{:S(2)}) collective-permute-start(bf16[1,24,2048]{2,1,0:T(8,128)(2,1)S(1)} %collective-permute-done.4), channel_id=1, source_target_pairs={{0,1},{1,2},{2,3},{3,4},{4,5},{5,6},{6,7},{7,8},{8,9},{9,10},{10,1... | collective-permute-start | bytes 294920 | tf_op jit(solution)/shard_map/ppermute | solution.py:36
  92.2 8.4 %collective-permute-start.7 = (bf16[1,24,2048]{2,1,0:T(8,128)(2,1)S(1)}, bf16[1,24,2048]{2,1,0:T(8,128)(2,1)S(1)}, u32[]{:S(2)}, u32[]{:S(2)}) collective-permute-start(bf16[1,24,2048]{2,1,0:T(8,128)(2,1)S(1)} %collective-permute-done.5), channel_id=1, source_target_pairs={{0,15},{1,0},{2,1},{3,2},{4,3},{5,4},{6,5},{7,6},{8,7},{9,8},{10,9... | collective-permute-start | bytes 294920 | tf_op jit(solution)/shard_map/ppermute | solution.py:41
  98.7 8.4 %collective-permute-start.8 = (bf16[1,24,2048]{2,1,0:T(8,128)(2,1)S(1)}, bf16[1,24,2048]{2,1,0:T(8,128)(2,1)S(1)}, u32[]{:S(2)}, u32[]{:S(2)}) collective-permute-start(bf16[1,24,2048]{2,1,0:T(8,128)(2,1)S(1)} %collective-permute-done.6), channel_id=1, source_target_pairs={{0,1},{1,2},{2,3},{3,4},{4,5},{5,6},{6,7},{7,8},{8,9},{9,10},{10,1... | collective-permute-start | bytes 294920 | tf_op jit(solution)/shard_map/ppermute | solution.py:36
  100.6 8.4 %collective-permute-start.9 = (bf16[1,24,2048]{2,1,0:T(8,128)(2,1)S(1)}, bf16[1,24,2048]{2,1,0:T(8,128)(2,1)S(1)}, u32[]{:S(2)}, u32[]{:S(2)}) collective-permute-start(bf16[1,24,2048]{2,1,0:T(8,128)(2,1)S(1)} %collective-permute-done.7), channel_id=1, source_target_pairs={{0,15},{1,0},{2,1},{3,2},{4,3},{5,4},{6,5},{7,6},{8,7},{9,8},{10,9... | collective-permute-start | bytes 294920 | tf_op jit(solution)/shard_map/ppermute | solution.py:41
  107.1 8.4 %collective-permute-start.10 = (bf16[1,24,2048]{2,1,0:T(8,128)(2,1)S(1)}, bf16[1,24,2048]{2,1,0:T(8,128)(2,1)S(1)}, u32[]{:S(2)}, u32[]{:S(2)}) collective-permute-start(bf16[1,24,2048]{2,1,0:T(8,128)(2,1)S(1)} %collective-permute-done.8), channel_id=1, source_target_pairs={{0,1},{1,2},{2,3},{3,4},{4,5},{5,6},{6,7},{7,8},{8,9},{9,10},{10,1... | collective-permute-start | bytes 294920 | tf_op jit(solution)/shard_map/ppermute | solution.py:36
  109.0 8.4 %collective-permute-start.11 = (bf16[1,24,2048]{2,1,0:T(8,128)(2,1)S(1)}, bf16[1,24,2048]{2,1,0:T(8,128)(2,1)S(1)}, u32[]{:S(2)}, u32[]{:S(2)}) collective-permute-start(bf16[1,24,2048]{2,1,0:T(8,128)(2,1)S(1)} %collective-permute-done.9), channel_id=1, source_target_pairs={{0,15},{1,0},{2,1},{3,2},{4,3},{5,4},{6,5},{7,6},{8,7},{9,8},{10,9... | collective-permute-start | bytes 294920 | tf_op jit(solution)/shard_map/ppermute | solution.py:41
  115.4 8.4 %collective-permute-start.12 = (bf16[1,24,2048]{2,1,0:T(8,128)(2,1)S(1)}, bf16[1,24,2048]{2,1,0:T(8,128)(2,1)S(1)}, u32[]{:S(2)}, u32[]{:S(2)}) collective-permute-start(bf16[1,24,2048]{2,1,0:T(8,128)(2,1)S(1)} %collective-permute-done.10), channel_id=1, source_target_pairs={{0,1},{1,2},{2,3},{3,4},{4,5},{5,6},{6,7},{7,8},{8,9},{9,10},{10,1... | collective-permute-start | bytes 294920 | tf_op jit(solution)/shard_map/ppermute | solution.py:36
  117.4 9.0 %collective-permute-start.13 = (bf16[1,24,2048]{2,1,0:T(8,128)(2,1)S(1)}, bf16[1,24,2048]{2,1,0:T(8,128)(2,1)S(1)}, u32[]{:S(2)}, u32[]{:S(2)}) collective-permute-start(bf16[1,24,2048]{2,1,0:T(8,128)(2,1)S(1)} %collective-permute-done.11), channel_id=1, source_target_pairs={{0,15},{1,0},{2,1},{3,2},{4,3},{5,4},{6,5},{7,6},{8,7},{9,8},{10,9... | collective-permute-start | bytes 294920 | tf_op jit(solution)/shard_map/ppermute | solution.py:41
  123.8 7.7 %collective-permute-start.14 = (bf16[1,24,2048]{2,1,0:T(8,128)(2,1)S(1)}, bf16[1,24,2048]{2,1,0:T(8,128)(2,1)S(1)}, u32[]{:S(2)}, u32[]{:S(2)}) collective-permute-start(bf16[1,24,2048]{2,1,0:T(8,128)(2,1)S(1)} %collective-permute-done.12), channel_id=1, source_target_pairs={{0,1},{1,2},{2,3},{3,4},{4,5},{5,6},{6,7},{7,8},{8,9},{9,10},{10,1... | collective-permute-start | bytes 294920 | tf_op jit(solution)/shard_map/ppermute | solution.py:36
  146.4 18.5 %all-to-all-start = ((bf16[32,128,4,24]{1,3,2,0:T(8,128)(2,1)}), bf16[32,128,4,24]{1,3,2,0:T(8,128)(2,1)S(1)}, u32[]{:S(2)}, u32[]{:S(2)}) async-start(bf16[32,128,4,24]{1,3,2,0:T(8,128)(2,1)} %copy.25), calls=%async_computation | async-start | bytes 1572864 | tf_op jit(solution)/shard_map/all_to_all | solution.py:72
  168.4 18.0 %all-to-all-start.1 = ((bf16[32,128,4,24]{1,3,2,0:T(8,128)(2,1)}), bf16[32,128,4,24]{1,3,2,0:T(8,128)(2,1)S(1)}, u32[]{:S(2)}, u32[]{:S(2)}) async-start(bf16[32,128,4,24]{1,3,2,0:T(8,128)(2,1)} %copy.29), calls=%async_computation.1 | async-start | bytes 1572864 | tf_op jit(solution)/shard_map/all_to_all | solution.py:56
  174.4 97.7 %reduce-scatter.2.cloned.1.call-start = ((), (), s32[]{:S(2)}) async-start(), calls=%async_computation.4 | async-start | bytes 1671168 | tf_op jit(solution)/shard_map/reduce_scatter | solution.py:80
  188.0 1.1 copy-start.3
  202.7 1.1 copy-start
Sparse Core Ops, SparseCore 0:
  11.1 92.3 all-gather.1
  202.9 69.1 reduce-scatter.1
